TPU v7x, 32 devices: a whole 2x2x4 slice. The times are simulated.
32 devices in a mesh: section: 2 (over core), dp: 16 (over z, y, x).
Axes of the slice: x: 2, y: 2, z: 4, core: 2. Of those that a mesh axis runs over, the one named last changes fastest.
Arguments:
- acts: bfloat16 [2, 16, 1, 64, 2, 2, 128], P('section', 'dp'), may hold values from -6 to 6
- preacts: bfloat16 [2, 16, 1, 64, 2, 2, 128], P('section', 'dp'), may hold values from -6 to 6
- top_grad: bfloat16 [16, 1, 64, 2, 2, 128], P('dp'), may hold values from -6 to 6
- weights: bfloat16 [2, 64, 1728], P('section'), may hold values from -0.21875 to 0.21875
- a_factor: bfloat16 [2, 1728, 1728], P('section', 'dp'), as said below
- g_factor: bfloat16 [2, 64, 64], P('section'), as said below
Outputs:
- act_grads: bfloat16 [2, 16, 1, 64, 2, 2, 128], P('section', 'dp')
- update: float32 [2, 1728, 64], P('section', 'dp')
- inverse: float32 [2, 1728, 1728], P('section', 'dp')
Inputs may be any that keep to these rules, and one draw needn't show every extreme that they name: `a_factor`: each matrix is symmetric and positive definite. `g_factor`: each matrix is symmetric and positive definite.
All inputs are finite; a program needn't handle non-finite values. Where the computation divides by a largest or mean magnitude, that divisor is 1e-20 or more.
Results may differ from a plain program's by a relative error of at most 0.006.
Values may be sent and summed in bfloat16 or wider, within the bound.
No kernel may reach another device: no remote copies, remote signals or barrier semaphores. Data moves between devices by JAX's collectives and lax.ppermute only.
A program may use at most 64 MiB of HBM per device.

v0:
```python
import jax
import jax.numpy as jnp
from jax import lax
from jax.sharding import PartitionSpec as P

KW = 3
MICRO = 1


def shifted(value, axis, steps):
    count = lax.axis_size(axis)
    first, last = (max(0, -steps), min(count, count - steps))
    return lax.ppermute(value, axis, [(source, source + steps) for source in range(first, last)])


def tap_offsets(kernel_width):
    middle = kernel_width // 2
    result = []
    for along_x in range(kernel_width):
        for along_y in range(kernel_width):
            for along_z in range(kernel_width):
                result.append((along_x - middle, along_y - middle, along_z - middle))
    return result


def taps_stack(volume, kernel_width, direction):
    middle = kernel_width // 2
    padded = jnp.pad(volume, ((0, 0), (middle, middle), (middle, middle), (middle, middle)))
    size_x, size_y, size_z = (volume.shape[1], volume.shape[2], volume.shape[3])
    pieces = []
    for off_x, off_y, off_z in tap_offsets(kernel_width):
        start_x = middle + direction * off_x
        start_y = middle + direction * off_y
        start_z = middle + direction * off_z
        pieces.append(
            padded[
                :,
                start_x : start_x + size_x,
                start_y : start_y + size_y,
                start_z : start_z + size_z,
            ]
        )
    stacked = jnp.stack(pieces, 0)
    return stacked.reshape(len(pieces) * volume.shape[0], size_x * size_y * size_z)


def back_input(grad_out, w_rows):
    columns = taps_stack(grad_out, KW, -1)
    summed = lax.dot_general(
        w_rows, columns, (((0,), (0,)), ((), ())), preferred_element_type=jnp.float32
    )
    return summed.astype(jnp.bfloat16).reshape(grad_out.shape)


def back_weight(volume, grad_out):
    columns = taps_stack(volume, KW, 1)
    flattened = grad_out.reshape(grad_out.shape[0], -1)
    return lax.dot_general(
        columns, flattened, (((1,), (1,)), ((), ())), preferred_element_type=jnp.float32
    )


def local_inverse(matrix):
    values = matrix.astype(jnp.float32)
    step_size = 1.0 / jnp.max(jnp.sum(jnp.abs(values), axis=1))
    identity = jnp.eye(matrix.shape[0], dtype=jnp.float32)
    resid0 = (identity - step_size * values).astype(jnp.bfloat16)
    resid1 = jnp.dot(resid0, resid0, preferred_element_type=jnp.float32).astype(jnp.bfloat16)
    cross_term = jnp.dot(resid1, resid0, preferred_element_type=jnp.float32)
    return step_size * (
        identity + resid0.astype(jnp.float32) + resid1.astype(jnp.float32) + cross_term
    )


def eye_rows(start_row, row_total, order_full):
    column_ids = lax.broadcasted_iota(jnp.int32, (row_total, order_full), 1)
    row_ids = lax.broadcasted_iota(jnp.int32, (row_total, order_full), 0)
    return (column_ids == start_row + row_ids).astype(jnp.float32)


def doubling_sum(value, axis):
    count = lax.axis_size(axis)
    assert count & count - 1 == 0
    stride = 1
    while stride < count:
        value = value + lax.ppermute(value, axis, [(i, i ^ stride) for i in range(count)])
        stride *= 2
    return value


def shards(acts, preacts, top_grad, weights, a_factor, g_factor):
    section_index = lax.axis_index("section")
    section_count = lax.axis_size("section")
    tick_count = MICRO + section_count - 1
    gathered = lax.all_gather(a_factor[0], "dp", axis=0, tiled=True)
    inputs = acts[0, 0]
    pre_values = preacts[0, 0]
    upper_grads = top_grad[0]
    channels = weights.shape[1]
    w_rows = weights[0].reshape(channels, -1, channels).transpose(1, 0, 2).reshape(-1, channels)
    zero_field = jnp.zeros(inputs.shape[1:], jnp.bfloat16)

    def one_tick(tick_index, carried):
        outgoing, stored_grads, stored_slopes = carried
        incoming = shifted(outgoing, "section", -1)
        micro_index = tick_index - (section_count - 1 - section_index)
        is_valid = jnp.logical_and(micro_index >= 0, micro_index < MICRO)
        clipped = jnp.clip(micro_index, 0, MICRO - 1)
        from_top = lax.dynamic_index_in_dim(upper_grads, clipped, 0, keepdims=False)
        arriving = jnp.where(section_index == section_count - 1, from_top, incoming)
        pre_now = lax.dynamic_index_in_dim(pre_values, clipped, 0, keepdims=False)
        grad_out = jnp.where(pre_now > 0, arriving, zero_field)
        sending = back_input(grad_out, w_rows)
        old_grad = lax.dynamic_index_in_dim(stored_grads, clipped, 0, keepdims=False)
        old_slope = lax.dynamic_index_in_dim(stored_slopes, clipped, 0, keepdims=False)
        stored_grads = lax.dynamic_update_index_in_dim(
            stored_grads, jnp.where(is_valid, sending, old_grad), clipped, 0
        )
        stored_slopes = lax.dynamic_update_index_in_dim(
            stored_slopes, jnp.where(is_valid, grad_out, old_slope), clipped, 0
        )
        return (sending, stored_grads, stored_slopes)

    start_state = (
        zero_field,
        jnp.zeros(inputs.shape, jnp.bfloat16),
        jnp.zeros(inputs.shape, jnp.bfloat16),
    )
    last_sent, stored_grads, stored_slopes = lax.fori_loop(0, tick_count, one_tick, start_state)
    local_grad = back_weight(inputs[0], stored_slopes[0])
    summed_grad = doubling_sum(local_grad, "dp")
    mean_grad = summed_grad / lax.axis_size("dp")
    a_rows = a_factor[0]
    row_total = a_rows.shape[0]
    order_full = a_rows.shape[1]
    first_row = lax.axis_index("dp") * row_total
    full_values = gathered.astype(jnp.float32)
    step_size = 1.0 / jnp.max(jnp.sum(jnp.abs(full_values), axis=1))
    full_resid0 = (jnp.eye(order_full, dtype=jnp.float32) - step_size * full_values).astype(
        jnp.bfloat16
    )
    own_eye = eye_rows(first_row, row_total, order_full)
    resid0 = (own_eye - step_size * a_rows.astype(jnp.float32)).astype(jnp.bfloat16)
    resid1 = jnp.dot(resid0, full_resid0, preferred_element_type=jnp.float32).astype(jnp.bfloat16)
    cross_term = jnp.dot(resid1, full_resid0, preferred_element_type=jnp.float32)
    inverse_rows = step_size * (
        own_eye + resid0.astype(jnp.float32) + resid1.astype(jnp.float32) + cross_term
    )
    g_inverse = local_inverse(g_factor[0])
    preconditioned = jnp.dot(
        mean_grad, g_inverse, precision=lax.Precision.HIGHEST, preferred_element_type=jnp.float32
    )
    update_rows = jnp.dot(
        inverse_rows,
        preconditioned,
        precision=lax.Precision.HIGHEST,
        preferred_element_type=jnp.float32,
    )
    return (stored_grads[None, None], update_rows[None], inverse_rows[None])


def solution(mesh):
    placed = (
        P("section", "dp", None, None, None, None, None),
        P("section", "dp", None, None, None, None, None),
        P("dp", None, None, None, None, None),
        P("section", None, None),
        P("section", "dp", None),
        P("section", None, None),
    )
    return jax.shard_map(
        shards,
        mesh=mesh,
        in_specs=placed,
        out_specs=(
            P("section", "dp", None, None, None, None, None),
            P("section", "dp", None),
            P("section", "dp", None),
        ),
        check_vma=False,
    )
```

profile of v0, /device:TPU:7, one launch (start us, length us, event | category | flops | bytes accessed | tf_op | source)
XLA Modules:
  0.0 239.3 jit_solution(13392514546595699222)
XLA Ops:
  7.2 2.5 %copy.17 = bf16[1,108,1728]{2,0,1:T(2,128)(2,1)} copy(bf16[1,108,1728]{2,1,0:T(8,128)(2,1)} %param.12) | data formatting | bytes 746496 | tf_op args[4]
  14.6 2.3 reshape.66
  18.2 24.4 %while.20 = (s32[]{:T(128)}, bf16[64,2,2,128]{3,2,1,0:T(2,128)(2,1)}, bf16[1,64,2,2,128]{4,3,2,1,0:T(2,128)(2,1)}, bf16[1,64,2,2,128]{4,3,2,1,0:T(2,128)(2,1)}, ...) while((s32[]{:T(128)}, ...), condition=%wide.region_1.2_spmd.clone, body=%wide.region_0.1_spmd.clone.sunk | while | flops 113475592 | bytes 10772739 | solution.py:129
  18.2 2.6 %collective-permute-start = (bf16[64,2,2,128]{3,2,1,0:T(2,128)(2,1)}, bf16[64,2,2,128]{3,2,1,0:T(2,128)(2,1)S(1)}, u32[]{:S(2)}, u32[]{:S(2)}) collective-permute-start(bf16[64,2,2,128]{3,2,1,0:T(2,128)(2,1)} %get-tuple-element.362), channel_id=1, source_target_pairs={{16,0},{17,1},{18,2},{19,3},{20,4},{21,5},{22,6},{23,7},{24,8},{25... | collective-permute-start | bytes 196616 | tf_op jit(solution)/shard_map/while/body/eval_jaxpr/ppermute | solution.py:13
  20.8 1.1 collective-permute-done
  21.9 1.7 fusion.172
  27.7 1.5 fusion.199
  30.6 2.2 collective-permute-start
  33.9 1.7 fusion.172
  39.7 1.5 fusion.199
  43.5 2.1 fusion.130
  45.9 21.8 %collective-permute-done.1 = f32[1728,64]{0,1:T(8,128)S(1)} collective-permute-done((f32[1728,64]{0,1:T(8,128)S(1)}, f32[1728,64]{0,1:T(8,128)S(1)}, u32[]{:S(2)}, u32[]{:S(2)}) %collective-permute-start.1) | collective-permute-done | bytes 442400 | tf_op jit(solution)/shard_map/ppermute | solution.py:86
  68.1 10.9 %collective-permute-done.2 = f32[1728,64]{0,1:T(8,128)S(1)} collective-permute-done((f32[1728,64]{0,1:T(8,128)S(1)}, f32[1728,64]{0,1:T(8,128)S(1)}, u32[]{:S(2)}, u32[]{:S(2)}) %collective-permute-start.2) | collective-permute-done | bytes 442400 | tf_op jit(solution)/shard_map/ppermute | solution.py:86
  79.1 1.2 collective-permute-start.3
  81.6 19.6 %collective-permute-done.3 = f32[1728,64]{0,1:T(8,128)S(1)} collective-permute-done((f32[1728,64]{0,1:T(8,128)S(1)}, f32[1728,64]{0,1:T(8,128)S(1)}, u32[]{:S(2)}, u32[]{:S(2)}) %collective-permute-start.3) | collective-permute-done | bytes 442400 | tf_op jit(solution)/shard_map/ppermute | solution.py:86
  101.3 2.3 collective-permute-start.4
  103.9 39.1 %collective-permute-done.4 = f32[1728,64]{0,1:T(8,128)S(1)} collective-permute-done((f32[1728,64]{0,1:T(8,128)S(1)}, f32[1728,64]{0,1:T(8,128)S(1)}, u32[]{:S(2)}, u32[]{:S(2)}) %collective-permute-start.4) | collective-permute-done | bytes 442400 | tf_op jit(solution)/shard_map/ppermute | solution.py:86
  143.5 48.4 %all-gather.3.cloned.1.call-done = bf16[1,1728,1728]{2,0,1:T(2,128)(2,1)} async-done(((bf16[1,108,1728]{2,0,1:T(2,128)(2,1)}), bf16[1,1728,1728]{2,0,1:T(2,128)(2,1)}) %all-gather.3.cloned.1.call-update) | async-done | bytes 5971984 | tf_op jit(solution)/shard_map/all_gather | solution.py:95
  191.9 18.9 %abs_reduce_fusion = f32[1728]{0:T(1024)S(1)} fusion(bf16[1,1728,1728]{2,0,1:T(2,128)(2,1)} %all-gather.3.cloned.1.call-done), kind=kLoop, calls=%fused_computation.89 | loop fusion | flops 8956224 | bytes 5978880 | tf_op jit(solution)/shard_map/reduce_sum | solution.py:138
  212.1 14.3 %convert_multiply_fusion = f32[1,1728,1728]{2,0,1:T(1,128)S(1)} fusion(bf16[1,1728,1728]{2,0,1:T(2,128)(2,1)} %all-gather.3.cloned.1.call-done, f32[]{:T(128)S(6)} %div.12), kind=kLoop, calls=%fused_computation.90 | loop fusion | flops 5971968 | bytes 17915908 | tf_op jit(solution)/shard_map/mul | solution.py:139
  226.5 1.3 convolution_convert_fusion.1
  227.8 1.4 fusion.55
  229.2 1.6 convolution_bitcast_fusion
  230.8 1.7 copy.18
  (126 shorter events, 21.9 us)
Async XLA Ops:
  7.2 2.7 %copy-start.4 = (bf16[1,64,1728]{2,1,0:T(8,128)(2,1)S(1)}, bf16[1,64,1728]{2,1,0:T(8,128)(2,1)}, u32[]{:S(2)}) copy-start(bf16[1,64,1728]{2,1,0:T(8,128)(2,1)} %param.11) | copy-start | bytes 663556
  7.2 4.1 %copy-start = (bf16[1,1,1,64,2,2,128]{6,5,4,3,2,1,0:T(2,128)(2,1)S(1)}, bf16[1,1,1,64,2,2,128]{6,5,4,3,2,1,0:T(2,128)(2,1)}, u32[]{:S(2)}) copy-start(bf16[1,1,1,64,2,2,128]{6,5,4,3,2,1,0:T(2,128)(2,1)} %param.8) | copy-start | bytes 196612
  7.2 184.7 %all-gather.3.cloned.1.call-start = ((), (), s32[]{:S(2)}) async-start(), calls=%async_computation | async-start | bytes 13160448 | tf_op jit(solution)/shard_map/all_gather | solution.py:95
  18.2 3.7 %collective-permute-start = (bf16[64,2,2,128]{3,2,1,0:T(2,128)(2,1)}, bf16[64,2,2,128]{3,2,1,0:T(2,128)(2,1)S(1)}, u32[]{:S(2)}, u32[]{:S(2)}) collective-permute-start(bf16[64,2,2,128]{3,2,1,0:T(2,128)(2,1)} %get-tuple-element.362), channel_id=1, source_target_pairs={{16,0},{17,1},{18,2},{19,3},{20,4},{21,5},{22,6},{23,7},{24,8},{25... | collective-permute-start | bytes 196616 | tf_op jit(solution)/shard_map/while/body/eval_jaxpr/ppermute | solution.py:13
  27.6 2.2 copy-start.2
  29.9 0.6 copy-start.3
  30.6 3.3 %collective-permute-start = (bf16[64,2,2,128]{3,2,1,0:T(2,128)(2,1)}, bf16[64,2,2,128]{3,2,1,0:T(2,128)(2,1)S(1)}, u32[]{:S(2)}, u32[]{:S(2)}) collective-permute-start(bf16[64,2,2,128]{3,2,1,0:T(2,128)(2,1)} %get-tuple-element.362), channel_id=1, source_target_pairs={{16,0},{17,1},{18,2},{19,3},{20,4},{21,5},{22,6},{23,7},{24,8},{25... | collective-permute-start | bytes 196616 | tf_op jit(solution)/shard_map/while/body/eval_jaxpr/ppermute | solution.py:13
  39.7 2.2 copy-start.2
  42.0 0.6 copy-start.3
  45.6 34.6 %copy-start.5 = (bf16[1,64,64]{2,1,0:T(8,128)(2,1)S(1)}, bf16[1,64,64]{2,1,0:T(8,128)(2,1)}, u32[]{:S(2)}) copy-start(bf16[1,64,64]{2,1,0:T(8,128)(2,1)} %param.13) | copy-start | bytes 24580
  45.6 22.1 %collective-permute-start.1 = (f32[1728,64]{0,1:T(8,128)S(1)}, f32[1728,64]{0,1:T(8,128)S(1)}, u32[]{:S(2)}, u32[]{:S(2)}) collective-permute-start(f32[1728,64]{0,1:T(8,128)S(1)} %fusion.130), channel_id=1, source_target_pairs={{0,1},{1,0},{2,3},{3,2},{4,5},{5,4},{6,7},{7,6},{8,9},{9,8},{10,11... | collective-permute-start | bytes 1327112 | tf_op jit(solution)/shard_map/ppermute | solution.py:86
  67.8 11.2 %collective-permute-start.2 = (f32[1728,64]{0,1:T(8,128)S(1)}, f32[1728,64]{0,1:T(8,128)S(1)}, u32[]{:S(2)}, u32[]{:S(2)}) collective-permute-start(f32[1728,64]{0,1:T(8,128)S(1)} %add.76), channel_id=1, source_target_pairs={{0,2},{1,3},{2,0},{3,1},{4,6},{5,7},{6,4},{7,5},{8,10},{9,11},{10,... | collective-permute-start | bytes 1327112 | tf_op jit(solution)/shard_map/ppermute | solution.py:86
  79.1 22.2 %collective-permute-start.3 = (f32[1728,64]{0,1:T(8,128)S(1)}, f32[1728,64]{0,1:T(8,128)S(1)}, u32[]{:S(2)}, u32[]{:S(2)}) collective-permute-start(f32[1728,64]{0,1:T(8,128)S(1)} %add.77), channel_id=1, source_target_pairs={{0,4},{1,5},{2,6},{3,7},{4,0},{5,1},{6,2},{7,3},{8,12},{9,13},{10,... | collective-permute-start | bytes 1327112 | tf_op jit(solution)/shard_map/ppermute | solution.py:86
  101.3 41.6 %collective-permute-start.4 = (f32[1728,64]{0,1:T(8,128)S(1)}, f32[1728,64]{0,1:T(8,128)S(1)}, u32[]{:S(2)}, u32[]{:S(2)}) collective-permute-start(f32[1728,64]{0,1:T(8,128)S(1)} %add.78), channel_id=1, source_target_pairs={{0,8},{1,9},{2,10},{3,11},{4,12},{5,13},{6,14},{7,15},{8,0},{9,1},... | collective-permute-start | bytes 1327112 | tf_op jit(solution)/shard_map/ppermute | solution.py:86
  212.1 14.3 %copy-start.1 = (bf16[1,108,1728]{2,1,0:T(8,128)(2,1)S(1)}, bf16[1,108,1728]{2,1,0:T(8,128)(2,1)}, u32[]{:S(2)}) copy-start(bf16[1,108,1728]{2,1,0:T(8,128)(2,1)} %param.12) | copy-start | bytes 1119748
Sparse Core Ops, SparseCore 0:
  11.4 180.4 all-gather.2
where the time goes:
time: 240 us; the launch traced here: 239 us
  waiting for transfers between devices  142 us (59%)
  other arithmetic  38.3 us (16%)
  local copies, waits for them, and re-layouts  24.1 us (10%)
  between operations  15.6 us (6%)
  matrix products  10.2 us (4%)
  starting transfers between devices  8.92 us (4%)
    ppermute x4, waiting for transfers between devices, doubling_sum(): lax.ppermute(value, axis, [(i, i ^ stride) for i in range(count)])  91.4 us
    all_gather x1, waiting for transfers between devices, shards(): gathered = lax.all_gather(a_factor[0], 'dp', axis=0, tiled=True)  48.4 us
    reduce_sum x1, other arithmetic, shards(): step_size = 1.0 / jnp.max(jnp.sum(jnp.abs(full_values), axis=1))  18.9 us
    mul x1, other arithmetic, shards(): step_size * full_values  14.3 us
    unnamed x37, local copies, waits for them, and re-layouts  8.38 us
    while x60, local copies, waits for them, and re-layouts  7.65 us
    ppermute x2, starting transfers between devices, shifted(): lax.ppermute(value, axis, [(source, source + steps) for source in range(f...  4.81 us
  transfers between devices with their start and end apart: 7, of which 7 were waited for; matrix products, arithmetic and copies ran while one was open for 12% of the time, Pallas kernels for 0%

commit v1 on v0

--- a/solution.py
+++ b/solution.py
@@ -92,7 +92,9 @@
     section_index = lax.axis_index("section")
     section_count = lax.axis_size("section")
     tick_count = MICRO + section_count - 1
-    gathered = lax.all_gather(a_factor[0], "dp", axis=0, tiled=True)
+    x = a_factor[0]
+    sent = jnp.stack([x] * lax.axis_size("dp"))
+    gathered = jnp.concatenate(lax.all_to_all(sent, "dp", 0, 0), axis=0)
     inputs = acts[0, 0]
     pre_values = preacts[0, 0]
     upper_grads = top_grad[0]

time: 240 us -> 229 us (0.954); the launches traced: 239 us -> 225 us
  local copies, waits for them, and re-layouts: 24.1 us -> 45.9 us
  other arithmetic: 38.3 us -> 21 us
  waiting for transfers between devices: 142 us -> 126 us
  between operations: 15.6 us -> 2.19 us
  matrix products: 10.2 us -> 17.1 us
  starting transfers between devices: 8.92 us -> 12.8 us
    all_gather x1 -> x0, waiting for transfers between devices: 48.4 us -> none  [shards(): gathered = lax.all_gather(a_factor[0], 'dp', axis=0, tiled=True)]
    ppermute x4, waiting for transfers between devices: 91.4 us -> 124 us  [doubling_sum(): lax.ppermute(value, axis, [(i, i ^ stride) for i in range(count)])]
    reduce_sum x1, other arithmetic: 18.9 us -> 4.21 us  [shards(): step_size = 1.0 / jnp.max(jnp.sum(jnp.abs(full_values), axis=1))]
    mul x0 -> x1, local copies, waits for them, and re-layouts: none -> 11.6 us  [shards(): step_size * full_values]
    convert_element_type x0 -> x1, local copies, waits for them, and re-layouts: none -> 8.77 us  [shards(): (jnp.eye(order_full, dtype=jnp.float32) - step_size * full_values).astype...]
    all_to_all x0 -> x1, starting transfers between devices: none -> 6.82 us  [shards(): gathered = jnp.concatenate(lax.all_to_all(sent, 'dp', 0, 0), axis=0)]
    dot_general x1, matrix products: 1.4 us -> 5.79 us  [shards(): jnp.dot(resid1, full_resid0, preferred_element_type=jnp.float32)]
    another operation x2 -> x3, local copies, waits for them, and re-layouts: 1.3 us -> 5.38 us  [the longest x1 4.07 us: shards(): sent = jnp.stack([x] * lax.axis_size('dp'))]
  transfers between devices with their start and end apart: 7 -> 7, of which waited for: 7 -> 6; matrix products, arithmetic and copies ran while one was open for 12% -> 13% of each run, Pallas kernels for 0% -> 0%
where the time goes in v1:
time: 229 us; the launch traced here: 225 us
  waiting for transfers between devices  126 us (55%)
  local copies, waits for them, and re-layouts  45.9 us (20%)
  other arithmetic  21 us (9%)
  matrix products  17.1 us (7%)
  starting transfers between devices  12.8 us (6%)
    ppermute x4, waiting for transfers between devices, doubling_sum(): lax.ppermute(value, axis, [(i, i ^ stride) for i in range(count)])  124 us
    mul x1, other arithmetic, shards(): step_size * full_values  11.7 us
    mul x1, local copies, waits for them, and re-layouts, shards(): step_size * full_values  11.6 us
    convert_element_type x1, local copies, waits for them, and re-layouts, shards(): (jnp.eye(order_full, dtype=jnp.float32) - step_size * full_values).astype...  8.77 us
    while x60, local copies, waits for them, and re-layouts  7.65 us
    all_to_all x1, starting transfers between devices, shards(): gathered = jnp.concatenate(lax.all_to_all(sent, 'dp', 0, 0), axis=0)  6.82 us
    unnamed x36, local copies, waits for them, and re-layouts  5.82 us
    dot_general x1, matrix products, shards(): jnp.dot(resid1, full_resid0, preferred_element_type=jnp.float32)  5.79 us
  transfers between devices with their start and end apart: 7, of which 6 were waited for; matrix products, arithmetic and copies ran while one was open for 13% of the time, Pallas kernels for 0%

profile of v1, /device:TPU:7, one launch (start us, length us, event | category | flops | bytes accessed | tf_op | source)
XLA Modules:
  0.0 225.4 jit_solution(13754976916206236490)
XLA Ops:
  0.6 4.1 %stack.367 = bf16[16,108,1728]{2,1,0:T(8,128)(2,1)} broadcast(bf16[108,1728]{1,0:T(8,128)(2,1)} %bitcast.353), dimensions={1,2} | broadcast | bytes 6345216 | tf_op jit(solution)/shard_map/stack | solution.py:96
  4.7 6.8 %all-to-all-start = ((bf16[16,108,1728]{2,1,0:T(8,128)(2,1)}), bf16[16,108,1728]{2,1,0:T(8,128)(2,1)}, u32[]{:S(2)}, u32[]{:S(2)}) async-start(bf16[16,108,1728]{2,1,0:T(8,128)(2,1)} %stack.367), calls=%async_computation | async-start | bytes 12845056 | tf_op jit(solution)/shard_map/all_to_all | solution.py:97
  16.3 2.1 reshape.110
  19.8 25.0 %while.20 = (s32[]{:T(128)}, bf16[64,2,2,128]{3,2,1,0:T(2,128)(2,1)}, bf16[1,64,2,2,128]{4,3,2,1,0:T(2,128)(2,1)}, bf16[1,64,2,2,128]{4,3,2,1,0:T(2,128)(2,1)}, ...) while((s32[]{:T(128)}, ...), condition=%wide.region_1.2_spmd.clone, body=%wide.region_0.1_spmd.clone.sunk | while | flops 113475592 | bytes 10772739 | solution.py:131
  19.8 3.1 %collective-permute-start = (bf16[64,2,2,128]{3,2,1,0:T(2,128)(2,1)}, bf16[64,2,2,128]{3,2,1,0:T(2,128)(2,1)S(1)}, u32[]{:S(2)}, u32[]{:S(2)}) collective-permute-start(bf16[64,2,2,128]{3,2,1,0:T(2,128)(2,1)} %get-tuple-element.364), channel_id=1, source_target_pairs={{16,0},{17,1},{18,2},{19,3},{20,4},{21,5},{22,6},{23,7},{24,8},{25... | collective-permute-start | bytes 196616 | tf_op jit(solution)/shard_map/while/body/eval_jaxpr/ppermute | solution.py:13
  23.0 1.1 collective-permute-done
  24.0 1.7 fusion.176
  29.8 1.5 fusion.203
  32.7 2.2 collective-permute-start
  36.1 1.7 fusion.176
  41.9 1.5 fusion.203
  45.6 2.1 fusion.133
  48.1 44.9 %collective-permute-done.1 = f32[1728,64]{0,1:T(8,128)S(1)} collective-permute-done((f32[1728,64]{0,1:T(8,128)S(1)}, f32[1728,64]{0,1:T(8,128)S(1)}, u32[]{:S(2)}, u32[]{:S(2)}) %collective-permute-start.1) | collective-permute-done | bytes 442400 | tf_op jit(solution)/shard_map/ppermute | solution.py:86
  93.2 16.7 %collective-permute-done.2 = f32[1728,64]{0,1:T(8,128)S(1)} collective-permute-done((f32[1728,64]{0,1:T(8,128)S(1)}, f32[1728,64]{0,1:T(8,128)S(1)}, u32[]{:S(2)}, u32[]{:S(2)}) %collective-permute-start.2) | collective-permute-done | bytes 442400 | tf_op jit(solution)/shard_map/ppermute | solution.py:86
  111.5 35.2 %collective-permute-done.3 = f32[1728,64]{0,1:T(8,128)S(1)} collective-permute-done((f32[1728,64]{0,1:T(8,128)S(1)}, f32[1728,64]{0,1:T(8,128)S(1)}, u32[]{:S(2)}, u32[]{:S(2)}) %collective-permute-start.3) | collective-permute-done | bytes 442400 | tf_op jit(solution)/shard_map/ppermute | solution.py:86
  147.1 27.2 %collective-permute-done.4 = f32[1728,64]{0,1:T(8,128)S(1)} collective-permute-done((f32[1728,64]{0,1:T(8,128)S(1)}, f32[1728,64]{0,1:T(8,128)S(1)}, u32[]{:S(2)}, u32[]{:S(2)}) %collective-permute-start.4) | collective-permute-done | bytes 442400 | tf_op jit(solution)/shard_map/ppermute | solution.py:86
  174.9 4.2 %fusion.54 = f32[16,108]{1,0:T(8,128)S(1)} fusion(bf16[16,108,1728]{2,1,0:T(8,128)(2,1)} %all-to-all-done), kind=kLoop, calls=%fused_computation.89 | loop fusion | flops 8956224 | bytes 5978880 | tf_op jit(solution)/shard_map/reduce_sum | solution.py:140
  180.4 11.7 %convert_multiply_fusion = (f32[16,108,1728]{2,1,0:T(8,128)}, bf16[16,108,1728]{2,1,0:T(8,128)(2,1)}) fusion(bf16[16,108,1728]{2,1,0:T(8,128)(2,1)} %all-to-all-done, f32[]{:T(128)S(6)} %div.12, s32[16,108]{1,0:T(8,128)S(1)} %multiply_add_fusion), kind=kLoop, calls=%fused_computation.87 | loop fusion | flops 17915904 | bytes 23894788 | tf_op jit(solution)/shard_map/mul | solution.py:141
  192.1 8.8 %convert_element_type.127 = bf16[1728,1728]{1,0:T(8,128)(2,1)} reshape(bf16[16,108,1728]{2,1,0:T(8,128)(2,1)} %get-tuple-element.292) | data formatting | bytes 11943936 | tf_op jit(solution)/shard_map/convert_element_type | solution.py:141
  200.8 11.6 %mul.52 = f32[1728,1728]{1,0:T(8,128)} reshape(f32[16,108,1728]{2,1,0:T(8,128)} %get-tuple-element.291) | data formatting | bytes 23887872 | tf_op jit(solution)/shard_map/mul | solution.py:141
  212.5 3.8 %convolution_convert_fusion.1 = bf16[108,1728]{1,0:T(8,128)(2,1)S(1)} fusion(bf16[1728,1728]{1,0:T(8,128)(2,1)} %convert_element_type.127, bf16[1,108,1728]{2,1,0:T(8,128)(2,1)S(1)} %copy-done.1, f32[]{:T(128)S(6)} %div.12, s32[108]{0:T(128)S(1)} %iota_add_fusion), kind=kOutput, calls=%fused_computation.123 | convolution fusion | flops 646278912 | bytes 6718900 | tf_op jit(solution)/shard_map/dot_general | solution.py:146
  216.3 5.8 %fusion.57 = f32[108,1728]{1,0:T(8,128)S(1)} fusion(bf16[108,1728]{1,0:T(8,128)(2,1)S(1)} %convolution_convert_fusion.1, f32[1728,1728]{1,0:T(8,128)} %mul.52, s32[108]{0:T(128)S(1)} %iota_add_fusion, f32[]{:T(128)S(6)} %div.12, bf16[1,108,1728]{2,1,0:T(8,128)(2,1)S(1)} %copy-done.1), kind=kOutput, calls=%fused_computation.122 | convolution fusion | flops 659155968 | bytes 13437364 | tf_op jit(solution)/shard_map/dot_general | solution.py:147
  222.1 1.6 convolution_bitcast_fusion
  223.7 1.7 copy.17
  (128 shorter events, 21.8 us)
Async XLA Ops:
  4.7 6.9 %copy-start.4 = (bf16[1,64,1728]{2,1,0:T(8,128)(2,1)S(1)}, bf16[1,64,1728]{2,1,0:T(8,128)(2,1)}, u32[]{:S(2)}) copy-start(bf16[1,64,1728]{2,1,0:T(8,128)(2,1)} %param.11) | copy-start | bytes 663556
  4.7 170.2 %all-to-all-start = ((bf16[16,108,1728]{2,1,0:T(8,128)(2,1)}), bf16[16,108,1728]{2,1,0:T(8,128)(2,1)}, u32[]{:S(2)}, u32[]{:S(2)}) async-start(bf16[16,108,1728]{2,1,0:T(8,128)(2,1)} %stack.367), calls=%async_computation | async-start | bytes 12845056 | tf_op jit(solution)/shard_map/all_to_all | solution.py:97
  11.5 1.5 copy-start
  19.8 4.2 %collective-permute-start = (bf16[64,2,2,128]{3,2,1,0:T(2,128)(2,1)}, bf16[64,2,2,128]{3,2,1,0:T(2,128)(2,1)S(1)}, u32[]{:S(2)}, u32[]{:S(2)}) collective-permute-start(bf16[64,2,2,128]{3,2,1,0:T(2,128)(2,1)} %get-tuple-element.364), channel_id=1, source_target_pairs={{16,0},{17,1},{18,2},{19,3},{20,4},{21,5},{22,6},{23,7},{24,8},{25... | collective-permute-start | bytes 196616 | tf_op jit(solution)/shard_map/while/body/eval_jaxpr/ppermute | solution.py:13
  29.8 2.2 copy-start.2
  32.1 0.6 copy-start.3
  32.7 3.3 %collective-permute-start = (bf16[64,2,2,128]{3,2,1,0:T(2,128)(2,1)}, bf16[64,2,2,128]{3,2,1,0:T(2,128)(2,1)S(1)}, u32[]{:S(2)}, u32[]{:S(2)}) collective-permute-start(bf16[64,2,2,128]{3,2,1,0:T(2,128)(2,1)} %get-tuple-element.364), channel_id=1, source_target_pairs={{16,0},{17,1},{18,2},{19,3},{20,4},{21,5},{22,6},{23,7},{24,8},{25... | collective-permute-start | bytes 196616 | tf_op jit(solution)/shard_map/while/body/eval_jaxpr/ppermute | solution.py:13
  41.8 2.2 copy-start.2
  44.1 0.6 copy-start.3
  47.8 62.3 %copy-start.5 = (bf16[1,64,64]{2,1,0:T(8,128)(2,1)S(1)}, bf16[1,64,64]{2,1,0:T(8,128)(2,1)}, u32[]{:S(2)}) copy-start(bf16[1,64,64]{2,1,0:T(8,128)(2,1)} %param.13) | copy-start | bytes 24580
  47.8 45.3 %collective-permute-start.1 = (f32[1728,64]{0,1:T(8,128)S(1)}, f32[1728,64]{0,1:T(8,128)S(1)}, u32[]{:S(2)}, u32[]{:S(2)}) collective-permute-start(f32[1728,64]{0,1:T(8,128)S(1)} %fusion.133), channel_id=1, source_target_pairs={{0,1},{1,0},{2,3},{3,2},{4,5},{5,4},{6,7},{7,6},{8,9},{9,8},{10,11... | collective-permute-start | bytes 1327112 | tf_op jit(solution)/shard_map/ppermute | solution.py:86
  93.1 16.8 %collective-permute-start.2 = (f32[1728,64]{0,1:T(8,128)S(1)}, f32[1728,64]{0,1:T(8,128)S(1)}, u32[]{:S(2)}, u32[]{:S(2)}) collective-permute-start(f32[1728,64]{0,1:T(8,128)S(1)} %add.80), channel_id=1, source_target_pairs={{0,2},{1,3},{2,0},{3,1},{4,6},{5,7},{6,4},{7,5},{8,10},{9,11},{10,... | collective-permute-start | bytes 1327112 | tf_op jit(solution)/shard_map/ppermute | solution.py:86
  110.0 36.7 %collective-permute-start.3 = (f32[1728,64]{0,1:T(8,128)S(1)}, f32[1728,64]{0,1:T(8,128)S(1)}, u32[]{:S(2)}, u32[]{:S(2)}) collective-permute-start(f32[1728,64]{0,1:T(8,128)S(1)} %add.81), channel_id=1, source_target_pairs={{0,4},{1,5},{2,6},{3,7},{4,0},{5,1},{6,2},{7,3},{8,12},{9,13},{10,... | collective-permute-start | bytes 1327112 | tf_op jit(solution)/shard_map/ppermute | solution.py:86
  146.8 27.5 %collective-permute-start.4 = (f32[1728,64]{0,1:T(8,128)S(1)}, f32[1728,64]{0,1:T(8,128)S(1)}, u32[]{:S(2)}, u32[]{:S(2)}) collective-permute-start(f32[1728,64]{0,1:T(8,128)S(1)} %add.82), channel_id=1, source_target_pairs={{0,8},{1,9},{2,10},{3,11},{4,12},{5,13},{6,14},{7,15},{8,0},{9,1},... | collective-permute-start | bytes 1327112 | tf_op jit(solution)/shard_map/ppermute | solution.py:86
  200.8 11.6 %copy-start.1 = (bf16[1,108,1728]{2,1,0:T(8,128)(2,1)S(1)}, bf16[1,108,1728]{2,1,0:T(8,128)(2,1)}, u32[]{:S(2)}) copy-start(bf16[1,108,1728]{2,1,0:T(8,128)(2,1)} %param.12) | copy-start | bytes 1119748
